TPU v7x, 512 devices: a whole 4x8x8 slice. The times are simulated.
512 devices in a mesh: tm: 64 (over y, x, core), head: 8 (over z).
Axes of the slice: x: 4, y: 8, z: 8, core: 2. Of those that a mesh axis runs over, the one named last changes fastest.
Arguments:
- queries: bfloat16 [24576, 5120], P('tm', 'head')
- keys: bfloat16 [24576, 5120], P('tm', 'head')
- values: bfloat16 [24576, 5120], P('tm', 'head')
- text_keys: bfloat16 [512, 5120], P('tm', 'head'), may hold values from -6 to 6
- text_values: bfloat16 [512, 5120], P('tm', 'head')
- out_weight: bfloat16 [5120, 5120], P('head', 'tm'), may hold values from -0.25 to 0.25
- windows: int32 [64], replicated, may hold values from 0 to 4, as said below
- lengths: int32 [64], replicated, may hold values from 96 to 384, as said below
Outputs:
- mixed: bfloat16 [24576, 5120], P('tm', 'head')
Inputs may be any that keep to these rules, and one draw needn't show every extreme that they name: windows reach 4 for some frame in every draw. `lengths`: some frame is full in every draw.
All inputs are finite; a program needn't handle non-finite values.
Results may differ from a plain program's by a relative error of at most 0.014.
Values may be sent and summed in bfloat16 or wider, within the bound.
No kernel may reach another device: no remote copies, remote signals or barrier semaphores. Data moves between devices by JAX's collectives and lax.ppermute only.
A program may use at most 64 MiB of HBM per device.

v0:
```python
import math
import jax
import jax.numpy as jnp
from jax import lax
from jax.sharding import PartitionSpec as P

HD = 128
WIN = 4


def from_behind(value, axis, steps):
    count = lax.axis_size(axis)
    initial, last = (max(0, -steps), min(count, count - steps))
    return lax.ppermute(value, axis, [(source, source + steps) for source in range(initial, last)])


def gather_text(text_keys, text_values):
    width = text_keys.shape[1]
    both = jnp.concatenate([text_keys, text_values], axis=1)
    full = lax.all_gather(both, "tm", axis=0, tiled=True)
    return (full[:, :width], full[:, width:])


def on_device(queries, keys, values, text_keys, text_values, out_weight, windows, lengths):
    rows = queries.shape[0]
    width = queries.shape[1]
    local_heads = width // HD
    groups = lax.axis_size("head")
    scale = 1.0 / math.sqrt(HD)
    position = lax.axis_index("tm")
    text_k, text_v = gather_text(text_keys, text_values)
    weight_all = lax.all_gather(out_weight, "tm", axis=1, tiled=True)
    kv = jnp.stack([keys, values])
    kv_list = [kv]
    for step in range(1, WIN + 1):
        kv_list.append(from_behind(kv, "tm", step))
    token_ids = jnp.arange(rows, dtype=jnp.int32)
    own_window = windows[position]
    mask_list = []
    for step in range(WIN + 1):
        source = position - step
        usable = (step <= own_window) & (source >= 0)
        source_len = lengths[jnp.maximum(source, 0)]
        mask_list.append(usable & (token_ids < source_len))
    mask_list.append(jnp.ones((text_k.shape[0],), bool))
    key_mask = jnp.concatenate(mask_list)
    all_keys = jnp.concatenate([p[0] for p in kv_list] + [text_k], axis=0)
    all_values = jnp.concatenate([p[1] for p in kv_list] + [text_v], axis=0)
    head_outputs = []
    for head_index in range(local_heads):
        lower = head_index * HD
        query_h = queries[:, lower : lower + HD]
        key_h = all_keys[:, lower : lower + HD]
        value_h = all_values[:, lower : lower + HD]
        scores = (
            lax.dot_general(
                query_h, key_h, (((1,), (1,)), ((), ())), preferred_element_type=jnp.float32
            )
            * scale
        )
        scores = jnp.where(key_mask[None, :], scores, -jnp.inf)
        top = jnp.max(scores, axis=-1, keepdims=True)
        weights = jnp.exp(scores - top)
        total = jnp.sum(weights, axis=-1, keepdims=True)
        attended = (
            jnp.dot(weights.astype(jnp.bfloat16), value_h, preferred_element_type=jnp.float32)
            / total
        )
        head_outputs.append(attended.astype(jnp.bfloat16))
    attended_all = jnp.concatenate(head_outputs, axis=1)
    w3 = weight_all.reshape(width, groups, weight_all.shape[1] // groups)
    partial_out = jnp.einsum("rk,kgc->grc", attended_all, w3, preferred_element_type=jnp.float32)
    mixed = lax.psum_scatter(
        partial_out.astype(jnp.bfloat16), "head", scatter_dimension=0, tiled=True
    )
    return mixed.reshape(rows, -1)


def solution(mesh):
    return jax.shard_map(
        on_device,
        mesh=mesh,
        in_specs=(
            P("tm", "head"),
            P("tm", "head"),
            P("tm", "head"),
            P("tm", "head"),
            P("tm", "head"),
            P("head", "tm"),
            P(),
            P(),
        ),
        out_specs=P("tm", "head"),
        check_vma=False,
    )
```

profile of v0, /device:TPU:1, one launch (start us, length us, event | category | flops | bytes accessed | tf_op | source)
XLA Modules:
  0.0 310.1 jit_solution(5613431030098832081)
XLA Ops:
  6.5 1.3 pad_maximum_fusion.1
  7.9 0.7 all-gather.5.cloned.1.call-update
  8.7 2.2 pad_maximum_fusion
  10.9 4.5 %collective-permute-start = (bf16[2,384,640]{2,1,0:T(8,128)(2,1)}, bf16[2,384,640]{2,1,0:T(8,128)(2,1)}, u32[]{:S(2)}, u32[]{:S(2)}) collective-permute-start(bf16[2,384,640]{2,1,0:T(8,128)(2,1)} %pad_maximum_fusion), channel_id=1, source_target_pairs={{0,8},{8,16},{16,24},{24,32},{32,40},{40,48},{48,56},{56,64},{64,7... | collective-permute-start | bytes 2949128 | tf_op jit(solution)/shard_map/ppermute | solution.py:14
  15.4 4.1 %collective-permute-start.1 = (bf16[2,384,640]{2,1,0:T(8,128)(2,1)}, bf16[2,384,640]{2,1,0:T(8,128)(2,1)}, u32[]{:S(2)}, u32[]{:S(2)}) collective-permute-start(bf16[2,384,640]{2,1,0:T(8,128)(2,1)} %pad_maximum_fusion), channel_id=1, source_target_pairs={{0,16},{8,24},{16,32},{24,40},{32,48},{40,56},{48,64},{56,72},{64,... | collective-permute-start | bytes 2949128 | tf_op jit(solution)/shard_map/ppermute | solution.py:14
  19.5 3.5 %collective-permute-start.2 = (bf16[2,384,640]{2,1,0:T(8,128)(2,1)}, bf16[2,384,640]{2,1,0:T(8,128)(2,1)}, u32[]{:S(2)}, u32[]{:S(2)}) collective-permute-start(bf16[2,384,640]{2,1,0:T(8,128)(2,1)} %pad_maximum_fusion), channel_id=1, source_target_pairs={{0,24},{8,32},{16,40},{24,48},{32,56},{40,64},{48,72},{56,80},{64,... | collective-permute-start | bytes 2949128 | tf_op jit(solution)/shard_map/ppermute | solution.py:14
  23.0 3.4 %collective-permute-start.3 = (bf16[2,384,640]{2,1,0:T(8,128)(2,1)}, bf16[2,384,640]{2,1,0:T(8,128)(2,1)}, u32[]{:S(2)}, u32[]{:S(2)}) collective-permute-start(bf16[2,384,640]{2,1,0:T(8,128)(2,1)} %pad_maximum_fusion), channel_id=1, source_target_pairs={{0,32},{8,40},{16,48},{24,56},{32,64},{40,72},{48,80},{56,88},{64,... | collective-permute-start | bytes 2949128 | tf_op jit(solution)/shard_map/ppermute | solution.py:14
  26.4 1.3 dynamic_slice.18
  30.9 1.5 fusion.104
  37.2 2.1 constant_dynamic-update-slice_fusion
  39.2 2.0 fusion.88
  41.3 11.2 %collective-permute-done.1 = bf16[2,384,640]{2,1,0:T(8,128)(2,1)} collective-permute-done((bf16[2,384,640]{2,1,0:T(8,128)(2,1)}, bf16[2,384,640]{2,1,0:T(8,128)(2,1)}, u32[]{:S(2)}, u32[]{:S(2)}) %collective-permute-start.1) | collective-permute-done | bytes 983072 | tf_op jit(solution)/shard_map/ppermute | solution.py:14
  52.4 2.0 fusion.87
  54.5 19.1 %collective-permute-done.2 = bf16[2,384,640]{2,1,0:T(8,128)(2,1)} collective-permute-done((bf16[2,384,640]{2,1,0:T(8,128)(2,1)}, bf16[2,384,640]{2,1,0:T(8,128)(2,1)}, u32[]{:S(2)}, u32[]{:S(2)}) %collective-permute-start.2) | collective-permute-done | bytes 983072 | tf_op jit(solution)/shard_map/ppermute | solution.py:14
  73.5 2.1 fusion.86
  75.6 14.6 %collective-permute-done.3 = bf16[2,384,640]{2,1,0:T(8,128)(2,1)} collective-permute-done((bf16[2,384,640]{2,1,0:T(8,128)(2,1)}, bf16[2,384,640]{2,1,0:T(8,128)(2,1)}, u32[]{:S(2)}, u32[]{:S(2)}) %collective-permute-start.3) | collective-permute-done | bytes 983072 | tf_op jit(solution)/shard_map/ppermute | solution.py:14
  90.2 2.1 fusion.85
  92.3 61.3 %all-gather.3.cloned.1.call-done = bf16[512,1280]{1,0:T(8,128)(2,1)} async-done(((bf16[8,1280]{1,0:T(8,128)(2,1)}), bf16[512,1280]{1,0:T(8,128)(2,1)}) %all-gather.3.cloned.1.call-update) | async-done | bytes 1310736 | tf_op jit(solution)/shard_map/all_gather | solution.py:20
  153.7 2.3 slice_dynamic-update-slice_fusion
  156.0 1.8 fusion.105
  158.4 0.9 fusion.106
  159.9 0.9 fusion.107
  161.5 0.9 fusion.108
  163.0 0.9 fusion.109
  164.5 1.9 fusion.72
  166.3 1.8 fusion.66
  168.2 1.9 fusion.60
  170.0 1.9 fusion.54
  171.9 1.9 fusion.48
  173.8 67.8 %all-gather.5.cloned.1.call-done = bf16[640,5120]{0,1:T(8,128)(2,1)} async-done(((bf16[640,80]{0,1:T(8,128)(2,1)}), bf16[640,5120]{0,1:T(8,128)(2,1)}) %all-gather.5.cloned.1.call-update) | async-done | bytes 6553616 | tf_op jit(solution)/shard_map/all_gather | solution.py:32
  241.6 8.9 %convert_bitcast_fusion = bf16[8,384,640]{2,1,0:T(8,128)(2,1)} fusion(bf16[640,8,640]{0,2,1:T(8,128)(2,1)} %bitcast.54, bf16[384,640]{1,0:T(8,128)(2,1)S(1)} %fusion.48), kind=kOutput, calls=%fused_computation.10 | convolution fusion | flops 2518548480 | bytes 10977280 | tf_op jit(solution)/shard_map/rk,kgc->grc/dot_general | solution.py:72
  250.5 53.1 %reduce-scatter.2.cloned.1.call-done = bf16[1,384,640]{2,1,0:T(8,128)(2,1)} async-done(((bf16[8,384,640]{2,1,0:T(8,128)(2,1)}), bf16[1,384,640]{2,1,0:T(8,128)(2,1)}) %reduce-scatter.2.cloned.1.call-update) | async-done | bytes 491536 | tf_op jit(solution)/shard_map/reduce_scatter | solution.py:73
  (26 shorter events, 8.0 us)
Async XLA Ops:
  6.5 147.1 %all-gather.3.cloned.1.call-start = ((), (), s32[]{:S(2)}) async-start(), calls=%async_computation.1 | async-start | bytes 1331200 | tf_op jit(solution)/shard_map/all_gather | solution.py:20
  7.9 233.7 %all-gather.5.cloned.1.call-start = ((), (), s32[]{:S(2)}) async-start(), calls=%async_computation.2 | async-start | bytes 6656000 | tf_op jit(solution)/shard_map/all_gather | solution.py:32
  8.6 294.9 %reduce-scatter.2.cloned.1.call-start = ((), (), s32[]{:S(2)}) async-start(), calls=%async_computation.3 | async-start | bytes 4423680 | tf_op jit(solution)/shard_map/reduce_scatter | solution.py:73
  10.9 28.3 %collective-permute-start = (bf16[2,384,640]{2,1,0:T(8,128)(2,1)}, bf16[2,384,640]{2,1,0:T(8,128)(2,1)}, u32[]{:S(2)}, u32[]{:S(2)}) collective-permute-start(bf16[2,384,640]{2,1,0:T(8,128)(2,1)} %pad_maximum_fusion), channel_id=1, source_target_pairs={{0,8},{8,16},{16,24},{24,32},{32,40},{40,48},{48,56},{56,64},{64,7... | collective-permute-start | bytes 2949128 | tf_op jit(solution)/shard_map/ppermute | solution.py:14
  15.4 37.0 %collective-permute-start.1 = (bf16[2,384,640]{2,1,0:T(8,128)(2,1)}, bf16[2,384,640]{2,1,0:T(8,128)(2,1)}, u32[]{:S(2)}, u32[]{:S(2)}) collective-permute-start(bf16[2,384,640]{2,1,0:T(8,128)(2,1)} %pad_maximum_fusion), channel_id=1, source_target_pairs={{0,16},{8,24},{16,32},{24,40},{32,48},{40,56},{48,64},{56,72},{64,... | collective-permute-start | bytes 2949128 | tf_op jit(solution)/shard_map/ppermute | solution.py:14
  19.5 54.0 %collective-permute-start.2 = (bf16[2,384,640]{2,1,0:T(8,128)(2,1)}, bf16[2,384,640]{2,1,0:T(8,128)(2,1)}, u32[]{:S(2)}, u32[]{:S(2)}) collective-permute-start(bf16[2,384,640]{2,1,0:T(8,128)(2,1)} %pad_maximum_fusion), channel_id=1, source_target_pairs={{0,24},{8,32},{16,40},{24,48},{32,56},{40,64},{48,72},{56,80},{64,... | collective-permute-start | bytes 2949128 | tf_op jit(solution)/shard_map/ppermute | solution.py:14
  23.0 67.2 %collective-permute-start.3 = (bf16[2,384,640]{2,1,0:T(8,128)(2,1)}, bf16[2,384,640]{2,1,0:T(8,128)(2,1)}, u32[]{:S(2)}, u32[]{:S(2)}) collective-permute-start(bf16[2,384,640]{2,1,0:T(8,128)(2,1)} %pad_maximum_fusion), channel_id=1, source_target_pairs={{0,32},{8,40},{16,48},{24,56},{32,64},{40,72},{48,80},{56,88},{64,... | collective-permute-start | bytes 2949128 | tf_op jit(solution)/shard_map/ppermute | solution.py:14
  156.0 2.5 copy-start
Sparse Core Ops, SparseCore 0:
  10.6 142.9 all-gather.2
  156.9 84.6 all-gather.4
  250.6 52.9 reduce-scatter.1
where the time goes:
time: 311 us; the launch traced here: 310 us
  waiting for transfers between devices  228 us (73%)
  matrix products  23.5 us (8%)
  local copies, waits for them, and re-layouts  17 us (5%)
  between operations  16.4 us (5%)
  starting transfers between devices  15.6 us (5%)
  other arithmetic  9.85 us (3%)
    all_gather x1, waiting for transfers between devices, on_device(): weight_all = lax.all_gather(out_weight, 'tm', axis=1, tiled=True)  67.8 us
    all_gather x1, waiting for transfers between devices, gather_text(): full = lax.all_gather(both, 'tm', axis=0, tiled=True)  61.3 us
    reduce_scatter x1, waiting for transfers between devices, on_device(): lax.psum_scatter(partial_out.astype(jnp.bfloat16), 'head', scatter_dimens...  53.1 us
    ppermute x4, waiting for transfers between devices, from_behind(): lax.ppermute(value, axis, [(source, source + steps) for source in range(i...  44.8 us
    ppermute x4, starting transfers between devices, from_behind(): lax.ppermute(value, axis, [(source, source + steps) for source in range(i...  15.5 us
    unnamed x12, local copies, waits for them, and re-layouts  11.6 us
    dot_general x5, matrix products, on_device(): jnp.dot(weights.astype(jnp.bfloat16), value_h, preferred_element_type=jnp...  9.3 us
    dot_general x1, matrix products, on_device(): jnp.einsum('rk,kgc->grc', attended_all, w3, preferred_element_type=jnp.fl...  8.89 us
  transfers between devices with their start and end apart: 7, of which 6 were waited for; matrix products, arithmetic and copies ran while one was open for 13% of the time, Pallas kernels for 0%

commit v1 on v0

--- a/solution.py
+++ b/solution.py
@@ -17,7 +17,8 @@
 def gather_text(text_keys, text_values):
     width = text_keys.shape[1]
     both = jnp.concatenate([text_keys, text_values], axis=1)
-    full = lax.all_gather(both, "tm", axis=0, tiled=True)
+    copies = jnp.concatenate([both] * lax.axis_size("tm"), axis=0)
+    full = lax.all_to_all(copies, "tm", 0, 0, tiled=True)
     return (full[:, :width], full[:, width:])
 
 

time: 311 us -> 296 us (0.952); the launches traced: 310 us -> 291 us
  waiting for transfers between devices: 228 us -> 174 us
  other arithmetic: 9.85 us -> 28.2 us
  starting transfers between devices: 15.6 us -> 26.4 us
  matrix products: 23.5 us -> 30.9 us
    all_gather x1 -> x0, waiting for transfers between devices: 61.3 us -> none  [gather_text(): full = lax.all_gather(both, 'tm', axis=0, tiled=True)]
    all_gather x1, waiting for transfers between devices: 67.8 us -> 8.45 us  [on_device(): weight_all = lax.all_gather(out_weight, 'tm', axis=1, tiled=True)]
    reduce_scatter x1, waiting for transfers between devices: 53.1 us -> 97.9 us  [on_device(): lax.psum_scatter(partial_out.astype(jnp.bfloat16), 'head', scatter_dimens...]
    unnamed x1 -> x64, other arithmetic: 0.01 us -> 21.8 us
    ppermute x4, waiting for transfers between devices: 44.8 us -> 66.5 us  [from_behind(): lax.ppermute(value, axis, [(source, source + steps) for source in range(i...]
    all_to_all x0 -> x1, starting transfers between devices: none -> 11.8 us  [gather_text(): full = lax.all_to_all(copies, 'tm', 0, 0, tiled=True)]
    dot_general x5, matrix products: 5.33 us -> 12.8 us  [on_device(): lax.dot_general(query_h, key_h, (((1,), (1,)), ((), ())), preferred_eleme...]
    unnamed x12 -> x26, local copies, waits for them, and re-layouts: 11.6 us -> 12.4 us
  transfers between devices with their start and end apart: 7 -> 7, of which waited for: 6 -> 6; matrix products, arithmetic and copies ran while one was open for 13% -> 22% of each run, Pallas kernels for 0% -> 0%
where the time goes in v1:
time: 296 us; the launch traced here: 291 us
  waiting for transfers between devices  174 us (59%)
  matrix products  30.9 us (10%)
  other arithmetic  28.2 us (10%)
  starting transfers between devices  26.4 us (9%)
  between operations  17.1 us (6%)
  local copies, waits for them, and re-layouts  15.1 us (5%)
    reduce_scatter x1, waiting for transfers between devices, on_device(): lax.psum_scatter(partial_out.astype(jnp.bfloat16), 'head', scatter_dimens...  97.9 us
    ppermute x4, waiting for transfers between devices, from_behind(): lax.ppermute(value, axis, [(source, source + steps) for source in range(i...  66.5 us
    unnamed x64, other arithmetic  21.8 us
    ppermute x4, starting transfers between devices, from_behind(): lax.ppermute(value, axis, [(source, source + steps) for source in range(i...  14.6 us
    dot_general x5, matrix products, on_device(): lax.dot_general(query_h, key_h, (((1,), (1,)), ((), ())), preferred_eleme...  12.8 us
    unnamed x26, local copies, waits for them, and re-layouts  12.4 us
    all_to_all x1, starting transfers between devices, gather_text(): full = lax.all_to_all(copies, 'tm', 0, 0, tiled=True)  11.8 us
    dot_general x5, matrix products, on_device(): jnp.dot(weights.astype(jnp.bfloat16), value_h, preferred_element_type=jnp...  9.17 us
  transfers between devices with their start and end apart: 7, of which 6 were waited for; matrix products, arithmetic and copies ran while one was open for 22% of the time, Pallas kernels for 0%

profile of v1, /device:TPU:1, one launch (start us, length us, event | category | flops | bytes accessed | tf_op | source)
XLA Modules:
  0.0 291.3 jit_solution(3928170729505915673)
XLA Ops:
  7.3 0.7 constant_dynamic-update-slice_fusion.63
  9.4 0.7 constant_dynamic-update-slice_fusion.60
  13.0 0.7 constant_dynamic-update-slice_fusion.55
  29.4 1.1 copy-done.4
  30.5 11.8 %all-to-all-start = ((bf16[64,8,1280]{2,1,0:T(8,128)(2,1)}), bf16[64,8,1280]{2,1,0:T(8,128)(2,1)S(1)}, u32[]{:S(2)}, u32[]{:S(2)}) async-start(bf16[64,8,1280]{2,1,0:T(8,128)(2,1)} %bitcast.57), calls=%async_computation | async-start | bytes 2621440 | tf_op jit(solution)/shard_map/all_to_all | solution.py:21
  42.5 3.5 %collective-permute-start = (bf16[2,384,640]{2,1,0:T(8,128)(2,1)S(1)}, bf16[2,384,640]{2,1,0:T(8,128)(2,1)}, u32[]{:S(2)}, u32[]{:S(2)}) collective-permute-start(bf16[2,384,640]{2,1,0:T(8,128)(2,1)S(1)} %pad_maximum_fusion), channel_id=1, source_target_pairs={{0,8},{8,16},{16,24},{24,32},{32,40},{40,48},{48,56},{56,64},{64,7... | collective-permute-start | bytes 2949128 | tf_op jit(solution)/shard_map/ppermute | solution.py:14
  46.0 4.1 %collective-permute-start.1 = (bf16[2,384,640]{2,1,0:T(8,128)(2,1)S(1)}, bf16[2,384,640]{2,1,0:T(8,128)(2,1)}, u32[]{:S(2)}, u32[]{:S(2)}) collective-permute-start(bf16[2,384,640]{2,1,0:T(8,128)(2,1)S(1)} %pad_maximum_fusion), channel_id=1, source_target_pairs={{0,16},{8,24},{16,32},{24,40},{32,48},{40,56},{48,64},{56,72},{64,... | collective-permute-start | bytes 2949128 | tf_op jit(solution)/shard_map/ppermute | solution.py:14
  50.1 3.6 %collective-permute-start.2 = (bf16[2,384,640]{2,1,0:T(8,128)(2,1)S(1)}, bf16[2,384,640]{2,1,0:T(8,128)(2,1)}, u32[]{:S(2)}, u32[]{:S(2)}) collective-permute-start(bf16[2,384,640]{2,1,0:T(8,128)(2,1)S(1)} %pad_maximum_fusion), channel_id=1, source_target_pairs={{0,24},{8,32},{16,40},{24,48},{32,56},{40,64},{48,72},{56,80},{64,... | collective-permute-start | bytes 2949128 | tf_op jit(solution)/shard_map/ppermute | solution.py:14
  53.6 3.4 %collective-permute-start.3 = (bf16[2,384,640]{2,1,0:T(8,128)(2,1)S(1)}, bf16[2,384,640]{2,1,0:T(8,128)(2,1)}, u32[]{:S(2)}, u32[]{:S(2)}) collective-permute-start(bf16[2,384,640]{2,1,0:T(8,128)(2,1)S(1)} %pad_maximum_fusion), channel_id=1, source_target_pairs={{0,32},{8,40},{16,48},{24,56},{32,64},{40,72},{48,80},{56,88},{64,... | collective-permute-start | bytes 2949128 | tf_op jit(solution)/shard_map/ppermute | solution.py:14
  66.2 1.0 constant_dynamic-update-slice_fusion.64
  67.3 13.3 %collective-permute-done = bf16[2,384,640]{2,1,0:T(8,128)(2,1)} collective-permute-done((bf16[2,384,640]{2,1,0:T(8,128)(2,1)S(1)}, bf16[2,384,640]{2,1,0:T(8,128)(2,1)}, u32[]{:S(2)}, u32[]{:S(2)}) %collective-permute-start) | collective-permute-done | bytes 983072 | tf_op jit(solution)/shard_map/ppermute | solution.py:14
  80.6 2.3 fusion.88
  82.9 24.2 %collective-permute-done.1 = bf16[2,384,640]{2,1,0:T(8,128)(2,1)} collective-permute-done((bf16[2,384,640]{2,1,0:T(8,128)(2,1)S(1)}, bf16[2,384,640]{2,1,0:T(8,128)(2,1)}, u32[]{:S(2)}, u32[]{:S(2)}) %collective-permute-start.1) | collective-permute-done | bytes 983072 | tf_op jit(solution)/shard_map/ppermute | solution.py:14
  107.1 2.2 fusion.87
  109.3 18.9 %collective-permute-done.2 = bf16[2,384,640]{2,1,0:T(8,128)(2,1)} collective-permute-done((bf16[2,384,640]{2,1,0:T(8,128)(2,1)S(1)}, bf16[2,384,640]{2,1,0:T(8,128)(2,1)}, u32[]{:S(2)}, u32[]{:S(2)}) %collective-permute-start.2) | collective-permute-done | bytes 983072 | tf_op jit(solution)/shard_map/ppermute | solution.py:14
  128.2 2.2 fusion.86
  130.5 10.0 %collective-permute-done.3 = bf16[2,384,640]{2,1,0:T(8,128)(2,1)} collective-permute-done((bf16[2,384,640]{2,1,0:T(8,128)(2,1)S(1)}, bf16[2,384,640]{2,1,0:T(8,128)(2,1)}, u32[]{:S(2)}, u32[]{:S(2)}) %collective-permute-start.3) | collective-permute-done | bytes 983072 | tf_op jit(solution)/shard_map/ppermute | solution.py:14
  140.5 2.2 fusion.85
  142.7 1.2 slice_dynamic-update-slice_fusion
  144.0 2.5 fusion.105
  147.1 2.5 fusion.106
  150.3 2.5 fusion.107
  153.5 2.5 fusion.108
  156.6 2.7 fusion.109
  160.0 1.8 fusion.72
  161.8 1.8 fusion.66
  163.7 1.8 fusion.60
  165.5 1.8 fusion.54
  167.3 1.8 fusion.48
  169.2 8.5 %all-gather.2.cloned.1.call-done = bf16[640,5120]{0,1:T(8,128)(2,1)} async-done(((bf16[640,80]{0,1:T(8,128)(2,1)}), bf16[640,5120]{0,1:T(8,128)(2,1)}) %all-gather.2.cloned.1.call-update) | async-done | bytes 6553616 | tf_op jit(solution)/shard_map/all_gather | solution.py:33
  177.6 8.9 %convert_bitcast_fusion = bf16[8,384,640]{2,1,0:T(8,128)(2,1)} fusion(bf16[640,8,640]{0,2,1:T(8,128)(2,1)} %bitcast.58, bf16[384,640]{1,0:T(8,128)(2,1)S(1)} %fusion.48), kind=kOutput, calls=%fused_computation.10 | convolution fusion | flops 2518548480 | bytes 10977280 | tf_op jit(solution)/shard_map/rk,kgc->grc/dot_general | solution.py:73
  186.5 97.9 %reduce-scatter.2.cloned.1.call-done = bf16[1,384,640]{2,1,0:T(8,128)(2,1)} async-done(((bf16[8,384,640]{2,1,0:T(8,128)(2,1)}), bf16[1,384,640]{2,1,0:T(8,128)(2,1)}) %reduce-scatter.2.cloned.1.call-update) | async-done | bytes 491536 | tf_op jit(solution)/shard_map/reduce_scatter | solution.py:74
  (102 shorter events, 29.6 us)
Async XLA Ops:
  6.5 22.4 %copy-start = (bf16[8,640]{1,0:T(8,128)(2,1)S(1)}, bf16[8,640]{1,0:T(8,128)(2,1)}, u32[]{:S(2)}) copy-start(bf16[8,640]{1,0:T(8,128)(2,1)} %param.12) | copy-start | bytes 30724
  6.5 22.4 %copy-start.1 = (bf16[8,640]{1,0:T(8,128)(2,1)S(1)}, bf16[8,640]{1,0:T(8,128)(2,1)}, u32[]{:S(2)}) copy-start(bf16[8,640]{1,0:T(8,128)(2,1)} %param.11) | copy-start | bytes 30724
  6.5 171.1 %all-gather.2.cloned.1.call-start = ((), (), s32[]{:S(2)}) async-start(), calls=%async_computation.2 | async-start | bytes 6656000 | tf_op jit(solution)/shard_map/all_gather | solution.py:33
  29.4 1.1 copy-start.4
  30.5 11.8 %copy-start.2 = (bf16[384,640]{1,0:T(8,128)(2,1)S(1)}, bf16[384,640]{1,0:T(8,128)(2,1)}, u32[]{:S(2)}) copy-start(bf16[384,640]{1,0:T(8,128)(2,1)} %param.9) | copy-start | bytes 1474564
  30.5 11.8 %copy-start.3 = (bf16[384,640]{1,0:T(8,128)(2,1)S(1)}, bf16[384,640]{1,0:T(8,128)(2,1)}, u32[]{:S(2)}) copy-start(bf16[384,640]{1,0:T(8,128)(2,1)} %param.10) | copy-start | bytes 1474564
  30.5 112.2 %all-to-all-start = ((bf16[64,8,1280]{2,1,0:T(8,128)(2,1)}), bf16[64,8,1280]{2,1,0:T(8,128)(2,1)S(1)}, u32[]{:S(2)}, u32[]{:S(2)}) async-start(bf16[64,8,1280]{2,1,0:T(8,128)(2,1)} %bitcast.57), calls=%async_computation | async-start | bytes 2621440 | tf_op jit(solution)/shard_map/all_to_all | solution.py:21
  42.3 14.8 %copy-start.7 = (s32[64]{0:T(128)S(1)}, s32[64]{0:T(128)}, u32[]{:S(2)}) copy-start(s32[64]{0:T(128)} %param.14) | copy-start | bytes 772
  42.3 18.6 %copy-start.6 = (s32[64]{0:T(128)S(1)}, s32[64]{0:T(128)}, u32[]{:S(2)}) copy-start(s32[64]{0:T(128)} %param.15) | copy-start | bytes 772
  42.3 242.2 %reduce-scatter.2.cloned.1.call-start = ((), (), s32[]{:S(2)}) async-start(), calls=%async_computation.3 | async-start | bytes 4423680 | tf_op jit(solution)/shard_map/reduce_scatter | solution.py:74
  42.5 38.1 %collective-permute-start = (bf16[2,384,640]{2,1,0:T(8,128)(2,1)S(1)}, bf16[2,384,640]{2,1,0:T(8,128)(2,1)}, u32[]{:S(2)}, u32[]{:S(2)}) collective-permute-start(bf16[2,384,640]{2,1,0:T(8,128)(2,1)S(1)} %pad_maximum_fusion), channel_id=1, source_target_pairs={{0,8},{8,16},{16,24},{24,32},{32,40},{40,48},{48,56},{56,64},{64,7... | collective-permute-start | bytes 2949128 | tf_op jit(solution)/shard_map/ppermute | solution.py:14
  46.0 61.1 %collective-permute-start.1 = (bf16[2,384,640]{2,1,0:T(8,128)(2,1)S(1)}, bf16[2,384,640]{2,1,0:T(8,128)(2,1)}, u32[]{:S(2)}, u32[]{:S(2)}) collective-permute-start(bf16[2,384,640]{2,1,0:T(8,128)(2,1)S(1)} %pad_maximum_fusion), channel_id=1, source_target_pairs={{0,16},{8,24},{16,32},{24,40},{32,48},{40,56},{48,64},{56,72},{64,... | collective-permute-start | bytes 2949128 | tf_op jit(solution)/shard_map/ppermute | solution.py:14
  50.1 78.1 %collective-permute-start.2 = (bf16[2,384,640]{2,1,0:T(8,128)(2,1)S(1)}, bf16[2,384,640]{2,1,0:T(8,128)(2,1)}, u32[]{:S(2)}, u32[]{:S(2)}) collective-permute-start(bf16[2,384,640]{2,1,0:T(8,128)(2,1)S(1)} %pad_maximum_fusion), channel_id=1, source_target_pairs={{0,24},{8,32},{16,40},{24,48},{32,56},{40,64},{48,72},{56,80},{64,... | collective-permute-start | bytes 2949128 | tf_op jit(solution)/shard_map/ppermute | solution.py:14
  53.6 86.9 %collective-permute-start.3 = (bf16[2,384,640]{2,1,0:T(8,128)(2,1)S(1)}, bf16[2,384,640]{2,1,0:T(8,128)(2,1)}, u32[]{:S(2)}, u32[]{:S(2)}) collective-permute-start(bf16[2,384,640]{2,1,0:T(8,128)(2,1)S(1)} %pad_maximum_fusion), channel_id=1, source_target_pairs={{0,32},{8,40},{16,48},{24,56},{32,64},{40,72},{48,80},{56,88},{64,... | collective-permute-start | bytes 2949128 | tf_op jit(solution)/shard_map/ppermute | solution.py:14
  142.7 1.2 copy-start.5
Sparse Core Ops, SparseCore 0:
  10.6 166.9 all-gather.1
  186.7 97.7 reduce-scatter.1
